TPU v7x, 32 devices: a whole 2x2x4 slice. The times are simulated.
32 devices in a mesh: groups: 2 (over y), lon: 8 (over z, x), lat: 2 (over core).
Axes of the slice: x: 2, y: 2, z: 4, core: 2. Of those that a mesh axis runs over, the one named last changes fastest.
Arguments:
- acts: bfloat16 [4, 96, 256, 256], P('groups', 'lat', 'lon'), parts along dimension 0, may hold values from -6 to 6
- rates: int32 [256], replicated, may hold values from 1 to 4, as said below
- dw_kernel: bfloat16 [9, 256], replicated, may hold values from -2 to 2
- pw_weight: bfloat16 [256, 256], replicated, may hold values from -0.375 to 0.375
- head_weight: bfloat16 [256, 227], replicated, may hold values from -0.375 to 0.375
- teacher_tiles: bfloat16 [512, 8, 227], P(('groups', 'lon', 'lat')), parts along dimension 0, may hold values from -6 to 6
- tile_dest: int32 [512, 1], P(('groups', 'lon', 'lat')), parts along dimension 0, may hold values from 0 to 15; in each aligned block of 16 rows (0 to 15, 16 to 31, ...) at most 2 rows name the same one
- tile_start: int32 [512], P(('groups', 'lon', 'lat')), parts along dimension 0, may hold values from 0 to 3064, as said below
- tile_count: int32 [512], P(('groups', 'lon', 'lat')), parts along dimension 0, may hold values from 1 to 8
Outputs:
- grad_dw: float32 [18, 256], P('groups'), parts along dimension 0
- grad_pw: float32 [512, 256], P('groups'), parts along dimension 0
- grad_head: float32 [512, 227], P('groups'), parts along dimension 0
- mse: float32 [2], P('groups'), parts along dimension 0
There are 2 independent parts, one for each index of `groups`. A program takes and returns all parts, laid end to end along the dimension named above; an argument that names none is the same for every part. Nothing has to cross between parts.
Inputs may be any that keep to these rules, and one draw needn't show every extreme that they name: The channels form 4 contiguous groups of 64 channels; all channels of a group share one rate, and the groups take the rates 1 to 4, each once, in an order that varies. `tile_dest`: among the 16 tiles of one teacher partition no destination is named more than 2 times. A tile's 8 cells lie in one row of one sample of its destination's block: tile_start mod 32 is at most 24.
All inputs are finite; a program needn't handle non-finite values.
Results may differ from a plain program's by a relative error of at most 0.0045.
Values may be sent and summed in bfloat16 or wider, within the bound.
No kernel may reach another device: no remote copies, remote signals or barrier semaphores. Data moves between devices by JAX's collectives and lax.ppermute only.
A program may use at most 64 MiB of HBM per device.

v0:
```python
import jax
import jax.numpy as jnp
from jax import lax
from jax.sharding import PartitionSpec as P

DMAX = 4
TILE = 8
CAP = 2


def padded_2(cells, sides, width, closed):
    for axis, dim in sides:
        count = lax.axis_size(axis)
        ends = count if closed else count - 1
        head = lax.slice_in_dim(cells, 0, width, axis=dim)
        tail = lax.slice_in_dim(cells, cells.shape[dim] - width, cells.shape[dim], axis=dim)
        cells = jnp.concatenate(
            [
                lax.ppermute(tail, axis, [(i, (i + 1) % count) for i in range(ends)]),
                cells,
                lax.ppermute(head, axis, [((i + 1) % count, i) for i in range(ends)]),
            ],
            axis=dim,
        )
    return cells


def tap_window(group_in, rate, tap_index, band_rows, block_cols):
    row_start = DMAX + (tap_index // 3 - 1) * rate
    col_start = DMAX + (tap_index % 3 - 1) * rate
    zero = jnp.int32(0)
    sizes = (group_in.shape[0], band_rows, block_cols, group_in.shape[3])
    return lax.dynamic_slice(group_in, (zero, row_start, col_start, zero), sizes)


def dilated(padded, kernel, rates, band_rows, block_cols):
    width = padded.shape[-1]
    group_width = width // DMAX
    outputs = []
    for group in range(DMAX):
        low = group * group_width
        group_in = padded[..., low : low + group_width]
        rate = rates[low]
        accum_sum = None
        for tap_index in range(9):
            window = tap_window(group_in, rate, tap_index, band_rows, block_cols)
            term = window.astype(jnp.float32) * kernel[tap_index, low : low + group_width]
            accum_sum = term if accum_sum is None else accum_sum + term
        outputs.append(accum_sum)
    return jnp.concatenate(outputs, axis=-1)


def dilated_grad(padded, grad_z, rates, band_rows, block_cols):
    width = padded.shape[-1]
    group_width = width // DMAX
    columns = []
    for group in range(DMAX):
        low = group * group_width
        group_in = padded[..., low : low + group_width]
        group_grad = grad_z[..., low : low + group_width]
        rate = rates[low]
        tap_sums = []
        for tap_index in range(9):
            window = tap_window(group_in, rate, tap_index, band_rows, block_cols)
            tap_sums.append(
                jnp.sum((window.astype(jnp.float32) * group_grad).reshape(-1, group_width), axis=0)
            )
        columns.append(jnp.stack(tap_sums, axis=0))
    return jnp.concatenate(columns, axis=1)


def local(
    acts, rates, dw_kernel, pw_weight, head_weight, teacher_tiles, tile_dest, tile_start, tile_count
):
    micro_batch, band_rows, block_cols, width = acts.shape
    teach_width = head_weight.shape[1]
    lat_index = lax.axis_index("lat")
    lat_count = lax.axis_size("lat")
    lon_count = lax.axis_size("lon")
    devices = lon_count * lat_count
    lon_padded = padded_2(acts, (("lon", 2),), DMAX, True)
    padded = padded_2(lon_padded, (("lat", 1),), DMAX, False)
    kernel = dw_kernel.astype(jnp.float32)
    depthwise_out = dilated(padded, kernel, rates, band_rows, block_cols).astype(jnp.bfloat16)
    depth_flat = depthwise_out.reshape(-1, width)
    preact = jnp.dot(depth_flat, pw_weight, preferred_element_type=jnp.float32)
    block_flat = (acts.reshape(-1, width).astype(jnp.float32) + jax.nn.silu(preact)).astype(
        jnp.bfloat16
    )
    tiles_here = teacher_tiles.shape[0]
    destination = tile_dest[:, 0]
    positions = jnp.arange(tiles_here, dtype=jnp.int32)
    same_dest = destination[:, None] == destination[None, :]
    earlier = positions[:, None] > positions[None, :]
    slot_rank = jnp.sum((same_dest & earlier).astype(jnp.int32), axis=1)
    slot_index = destination * CAP + slot_rank
    send_tiles = (
        jnp.zeros((devices * CAP, TILE, teach_width), jnp.bfloat16)
        .at[slot_index]
        .set(teacher_tiles)
    )
    send_start = jnp.zeros((devices * CAP,), jnp.int32).at[slot_index].set(tile_start)
    send_count = jnp.zeros((devices * CAP,), jnp.int32).at[slot_index].set(tile_count)
    recv_tiles, recv_start, recv_count = (
        lax.all_to_all(send_tiles, ("lon", "lat"), split_axis=0, concat_axis=0, tiled=True),
        lax.all_to_all(send_start, ("lon", "lat"), split_axis=0, concat_axis=0, tiled=True),
        lax.all_to_all(send_count, ("lon", "lat"), split_axis=0, concat_axis=0, tiled=True),
    )
    offsets = jnp.arange(TILE, dtype=jnp.int32)
    cell_index = recv_start[:, None] + offsets[None, :]
    is_valid = offsets[None, :] < recv_count[:, None]
    inner_row = recv_start // block_cols % band_rows
    glob_row = lat_index * band_rows + inner_row
    area_weight = jnp.cos(
        jnp.pi * ((glob_row.astype(jnp.float32) + 0.5) / (band_rows * lat_count) - 0.5)
    )
    row_weight = jnp.where(is_valid, area_weight[:, None], jnp.float32(0.0)) / jnp.float32(
        devices * tiles_here * TILE
    )
    row_weight = row_weight.reshape(-1, 1)
    cell_flat = cell_index.reshape(-1)
    y_rows = block_flat[cell_flat]
    predicted = jnp.dot(y_rows, head_weight, preferred_element_type=jnp.float32)
    residual = predicted - recv_tiles.reshape(-1, teach_width).astype(jnp.float32)
    loss_sum = jnp.sum(row_weight * residual * residual)
    grad_pred = (2.0 * row_weight * residual).astype(jnp.bfloat16)
    grad_head = lax.dot_general(
        y_rows, grad_pred, (((0,), (0,)), ((), ())), preferred_element_type=jnp.float32
    )
    grad_rows = jnp.dot(grad_pred, head_weight.T, preferred_element_type=jnp.float32)
    grad_y = jnp.zeros((block_flat.shape[0], width), jnp.float32).at[cell_flat].add(grad_rows)
    sigmoid_u = jax.nn.sigmoid(preact)
    grad_u = (grad_y * sigmoid_u * (1.0 + preact * (1.0 - sigmoid_u))).astype(jnp.bfloat16)
    grad_pw = lax.dot_general(
        depth_flat, grad_u, (((0,), (0,)), ((), ())), preferred_element_type=jnp.float32
    )
    grad_z = jnp.dot(grad_u, pw_weight.T, preferred_element_type=jnp.float32).reshape(
        micro_batch, band_rows, block_cols, width
    )
    grad_dw = dilated_grad(padded, grad_z, rates, band_rows, block_cols)
    grad_dw, grad_pw, grad_head, loss_sum = lax.psum(
        (grad_dw, grad_pw, grad_head, loss_sum), ("lon", "lat")
    )
    return (grad_dw, grad_pw, grad_head, (loss_sum / teach_width).reshape(1))


def solution(mesh):
    in_specs = (
        P("groups", "lat", "lon", None),
        P(),
        P(),
        P(),
        P(),
        P(("groups", "lon", "lat"), None, None),
        P(("groups", "lon", "lat"), None),
        P(("groups", "lon", "lat")),
        P(("groups", "lon", "lat")),
    )
    out_specs = (P("groups", None), P("groups", None), P("groups", None), P("groups"))
    return jax.shard_map(local, mesh=mesh, in_specs=in_specs, out_specs=out_specs, check_vma=False)
```

profile of v0, /device:TPU:8, one launch (start us, length us, event | category | flops | bytes accessed | tf_op | source)
XLA Modules:
  0.0 212.1 jit_solution(15716888762554736010)
XLA Ops:
  7.2 0.0 copy-start
  7.2 1.0 convert_reduce_fusion
  8.2 0.7 fusion.86
  8.8 0.8 scatter_custom_fusion.1
  9.6 0.7 all_to_all.17
  10.3 6.3 %all-to-all-start.1 = ((s32[16,2,1]{1,2,0:T(1,128)}), s32[16,2,1]{1,2,0:T(1,128)S(1)}, u32[]{:S(2)}, u32[]{:S(2)}) async-start(s32[16,2,1]{1,2,0:T(1,128)} %bitcast.8), calls=%async_computation.1 | async-start | bytes 16384 | tf_op jit(solution)/shard_map/all_to_all | solution.py:107
  16.5 1.3 fusion.94
  17.8 1.5 collective-permute-start
  19.3 1.5 collective-permute-start.1
  20.8 1.4 fusion.95
  32.8 0.7 convert_element_type.185
  33.5 0.1 slice_bitcast_fusion.34
  33.5 0.7 slice_bitcast_fusion.35
  34.2 0.8 scatter_custom_fusion
  35.1 0.7 all_to_all.15
  35.8 5.2 %all-to-all-start = ((s32[16,2,1]{1,2,0:T(1,128)}), s32[16,2,1]{1,2,0:T(1,128)S(1)}, u32[]{:S(2)}, u32[]{:S(2)}) async-start(s32[16,2,1]{1,2,0:T(1,128)} %bitcast.6), calls=%async_computation | async-start | bytes 16384 | tf_op jit(solution)/shard_map/all_to_all | solution.py:106
  41.0 0.7 broadcast_in_dim.15
  41.6 2.3 %scatter_fusion = bf16[32,8,227]{2,1,0:T(8,128)(2,1)} fusion(bf16[32,8,227]{2,1,0:T(8,128)(2,1)} %broadcast_in_dim.15, s32[16]{0:T(128)S(1)} %fusion.86, bf16[16,8,227]{2,1,0:T(8,128)(2,1)} %param.14), kind=kCustom, calls=%fused_computation.3 | custom fusion | bytes 174400 | tf_op jit(solution)/shard_map/scatter | solution.py:100
  43.9 0.6 broadcast.181
  44.5 0.6 reduce.43
  45.2 0.1 lt.50
  45.2 0.7 all-to-all-done
  45.9 5.4 %all-to-all-start.2 = ((bf16[32,8,227]{2,1,0:T(8,128)(2,1)}), bf16[32,8,227]{2,1,0:T(8,128)(2,1)S(1)}, u32[]{:S(2)}, u32[]{:S(2)}) async-start(bf16[32,8,227]{2,1,0:T(8,128)(2,1)} %scatter_fusion), calls=%async_computation.2 | async-start | bytes 262144 | tf_op jit(solution)/shard_map/all_to_all | solution.py:105
  51.3 0.0 all-reduce.4.cloned.1.call-start
  51.4 0.6 reduce.42
  52.0 0.1 add.555
  52.1 0.1 iota_add_fusion
  52.2 0.1 fusion.85
  52.3 0.1 add.559
  52.4 0.1 select_multiply_fusion
  52.4 0.1 div.43
  52.5 0.1 mul.598
  52.7 0.2 pad_maximum_fusion.4
  52.8 2.1 collective-permute-start.2
  54.9 1.3 collective-permute-start.3
  56.2 0.5 all-to-all-done.2
  56.8 0.1 copy.19
  56.9 1.3 collective-permute-done.3
  58.2 1.4 pad_maximum_fusion
  59.6 1.0 fusion.93
  60.6 0.3 copy-done.7
  61.0 3.5 %fusion.9 = bf16[2,48,32,64]{3,2,1,0:T(8,128)(2,1)S(1)} fusion(f32[64]{0:T(128)S(1)} %get-tuple-element.101, f32[64]{0:T(128)S(1)} %get-tuple-element.102, f32[64]{0:T(128)S(1)} %get-tuple-element.103, f32[64]{0:T(128)S(1)} %get-tuple-element.104, f32[64]{0:T(128)S(1)} %get-tuple-element.105, f32[64]{0:T(128)S(1)} %get-tuple-element.106, ...), kind=kLoop, calls=%fused_computation.90 | loop fusion | flops 5308416 | bytes 3934480 | tf_op jit(solution)/shard_map/convert.9
  64.6 3.1 %fusion.63 = bf16[2,48,32,64]{3,2,1,0:T(8,128)(2,1)S(1)} fusion(f32[64]{0:T(128)S(1)} %copy-done.22, f32[64]{0:T(128)S(1)} %copy-done.23, f32[64]{0:T(128)S(1)} %copy-done.24, f32[64]{0:T(128)S(1)} %copy-done.25, f32[64]{0:T(128)S(1)} %copy-done.26, f32[64]{0:T(128)S(1)} %copy-done.27, f32[64]{0:T(128)S(1)} %copy-done.28, f32[64]{0:T(128)S(1)} %copy-done.29, ...), kind=kLoop, calls=%fused_computation.144 | loop fusion | flops 5308416 | bytes 3934480 | tf_op jit(solution)/shard_map/convert.6
  67.8 3.5 %fusion.45 = bf16[2,48,32,64]{3,2,1,0:T(8,128)(2,1)S(1)} fusion(f32[64]{0:T(128)S(1)} %get-tuple-element.82, f32[64]{0:T(128)S(1)} %get-tuple-element.83, f32[64]{0:T(128)S(1)} %get-tuple-element.84, f32[64]{0:T(128)S(1)} %get-tuple-element.85, f32[64]{0:T(128)S(1)} %get-tuple-element.86, f32[64]{0:T(128)S(1)} %copy-done.18, f32[64]{0:T(128)S(1)} %copy-done.19, ...), kind=kLoop, calls=%fused_computation.126 | loop fusion | flops 5308416 | bytes 3934480 | tf_op jit(solution)/shard_map/convert.7
  71.3 3.3 %fusion.27 = bf16[2,48,32,64]{3,2,1,0:T(8,128)(2,1)S(1)} fusion(f32[64]{0:T(128)S(1)} %get-tuple-element.92, f32[64]{0:T(128)S(1)} %get-tuple-element.93, f32[64]{0:T(128)S(1)} %get-tuple-element.94, f32[64]{0:T(128)S(1)} %get-tuple-element.95, f32[64]{0:T(128)S(1)} %get-tuple-element.96, f32[64]{0:T(128)S(1)} %get-tuple-element.97, ...), kind=kLoop, calls=%fused_computation.108 | loop fusion | flops 5308416 | bytes 3934480 | tf_op jit(solution)/shard_map/convert.8
  74.7 3.4 %fusion = (bf16[3072,256]{1,0:T(8,128)(2,1)}, f32[3072,256]{1,0:T(8,128)}) fusion(bf16[2,48,32,256]{3,2,1,0:T(8,128)(2,1)S(1)} %copy-done.7, bf16[256,256]{1,0:T(8,128)(2,1)S(1)} %copy-done, bf16[3072,64]{1,0:T(8,128)(2,1)S(1)} %bitcast.171, bf16[3072,64]{1,0:T(8,128)(2,1)S(1)} %bitcast.173, bf16[3072,64]{1,0:T(8,128)(2,1)S(1)} %bitcast.175, ...), kind=kOutput, calls=%fused_computation.6 | convolution fusion | flops 414449664 | bytes 7995392 | tf_op jit(solution)/shard_map/dot_general | solution.py:86
  78.0 2.6 %gather_fusion = bf16[256,256]{1,0:T(8,128)(2,1)S(1)} fusion(bf16[3072,256]{1,0:T(8,128)(2,1)} %get-tuple-element.114, s32[1024]{0:T(1024)S(1)} %pad_clamp_fusion), kind=kCustom, calls=%fused_computation | custom fusion | bytes 263168 | tf_op jit(solution)/shard_map/gather | solution.py:122
  80.6 0.9 fusion.75
  81.5 0.9 fusion.76
  82.4 0.2 fusion.77
  82.6 3.8 %scatter_custom_fusion.3 = f32[3072,256]{1,0:T(8,128)} fusion(s32[256]{0:T(256)S(1)} %bitcast.178, f32[256,256]{1,0:T(8,128)S(1)} %fusion.77, f32[]{:T(128)} %constant.101.clone.1), kind=kCustom, calls=%fused_computation.155 | custom fusion | flops 65536 | bytes 3145732 | tf_op jit(solution)/shard_map/scatter-add | solution.py:131
  86.4 4.0 %multiply_convert_fusion = bf16[3072,256]{1,0:T(8,128)(2,1)S(1)} fusion(f32[3072,256]{1,0:T(8,128)} %get-tuple-element.115, f32[3072,256]{1,0:T(8,128)} %scatter_custom_fusion.3), kind=kLoop, calls=%fused_computation.7 | loop fusion | flops 7077888 | bytes 7864320 | tf_op jit(solution)/shard_map/convert_element_type | solution.py:133
  90.5 1.1 copy-done.8
  91.6 2.2 %fusion.91 = f32[256,256]{1,0:T(8,128)} fusion(bf16[3072,256]{1,0:T(8,128)(2,1)S(1)} %multiply_convert_fusion, bf16[3072,64]{1,0:T(8,128)(2,1)S(1)} %bitcast.172, bf16[3072,64]{1,0:T(8,128)(2,1)S(1)} %bitcast.174, bf16[3072,64]{1,0:T(8,128)(2,1)S(1)} %bitcast.176, bf16[3072,64]{1,0:T(8,128)(2,1)S(1)} %bitcast.170), kind=kOutput, calls=%fused_computation.232 | convolution fusion | flops 408944640 | bytes 3407872 | tf_op jit(solution)/shard_map/dot_general | solution.py:134
  93.8 2.1 %fusion.96 = f32[3072,256]{1,0:T(8,128)S(1)} fusion(bf16[3072,256]{1,0:T(8,128)(2,1)} %copy-done.8, bf16[256,256]{1,0:T(8,128)(2,1)S(1)} %copy-done), kind=kOutput, calls=%fused_computation.237 | convolution fusion | flops 402653184 | bytes 4849664 | tf_op jit(solution)/shard_map/dot_general | solution.py:137
  96.0 1.7 copy-done.5
  97.6 10.6 %fusion.18 = (f32[64]{0:T(128)S(1)}, f32[64]{0:T(128)S(1)}, f32[64]{0:T(128)S(1)}, f32[64]{0:T(128)S(1)}, f32[64]{0:T(128)S(1)}, /*index=5*/f32[64]{0:T(128)S(1)...) fusion(f32[2,48,32,256]{3,2,1,0:T(8,128)S(1)} %bitcast.167, ...), kind=kLoop, calls=%fused_computation.99 | loop fusion | flops 14154240 | bytes 11802672 | tf_op jit(solution)/shard_map/reduce_sum | solution.py:66
  108.2 0.0 all-reduce.4.cloned.1.call-update
  108.3 7.1 %fusion.36 = (f32[64]{0:T(128)S(1)}, f32[64]{0:T(128)S(1)}, f32[64]{0:T(128)S(1)}, f32[64]{0:T(128)S(1)}, f32[64]{0:T(128)S(1)}, /*index=5*/f32[64]{0:T(128)S(1)...) fusion(f32[2,48,32,256]{3,2,1,0:T(8,128)} %bitcast.168, ...), kind=kLoop, calls=%fused_computation.117 | loop fusion | flops 7077120 | bytes 7867408 | tf_op jit(solution)/shard_map/reduce_sum | solution.py:66
  115.5 0.1 pad_maximum_fusion.5
  115.6 53.6 %all-reduce = (f32[9,256]{1,0:T(8,128)}, f32[]{:T(128)}) all-reduce(f32[9,256]{1,0:T(8,128)S(1)} %pad_maximum_fusion.5, f32[]{:T(128)} %get-tuple-element.116), channel_id=1, replica_groups=mesh['groups'=2,'lon'=8,'lat'=2] {'lon','lat'}, use_global_device_ids=true, to_apply=%region_41.42 | all-reduce | flops 2305 | bytes 18440 | tf_op jit(solution)/shard_map/psum | solution.py:141
  169.9 31.0 %all-reduce.4.cloned.1.call-done = (f32[256,256]{1,0:T(8,128)}, f32[256,227]{0,1:T(8,128)}) async-done(((f32[256,256]{1,0:T(8,128)}, f32[256,227]{0,1:T(8,128)}), (f32[256,256]{1,0:T(8,128)}, f32[256,227]{0,1:T(8,128)})) %all-reduce.4.cloned.1.call-update) | async-done | bytes 494608 | tf_op jit(solution)/shard_map/psum | solution.py:141
  200.8 1.7 copy.23
  202.5 1.6 copy.24
  (71 shorter events, 0.3 us)
Async XLA Ops:
  7.2 67.5 %copy-start = (bf16[256,256]{1,0:T(8,128)(2,1)S(1)}, bf16[256,256]{1,0:T(8,128)(2,1)}, u32[]{:S(2)}) copy-start(bf16[256,256]{1,0:T(8,128)(2,1)} %param.12) | copy-start | bytes 393220
  7.2 45.5 %copy-start.6 = (bf16[2,48,32,256]{3,2,1,0:T(8,128)(2,1)S(1)}, bf16[2,48,32,256]{3,2,1,0:T(8,128)(2,1)}, u32[]{:S(2)}) copy-start(bf16[2,48,32,256]{3,2,1,0:T(8,128)(2,1)} %param.9) | copy-start | bytes 4718596
  10.3 25.5 %all-to-all-start.1 = ((s32[16,2,1]{1,2,0:T(1,128)}), s32[16,2,1]{1,2,0:T(1,128)S(1)}, u32[]{:S(2)}, u32[]{:S(2)}) async-start(s32[16,2,1]{1,2,0:T(1,128)} %bitcast.8), calls=%async_computation.1 | async-start | bytes 16384 | tf_op jit(solution)/shard_map/all_to_all | solution.py:107
  17.8 34.8 %collective-permute-start = (bf16[2,48,4,256]{3,2,1,0:T(4,128)(2,1)S(1)}, bf16[2,48,4,256]{3,2,1,0:T(4,128)(2,1)S(1)}, u32[]{:S(2)}, u32[]{:S(2)}) collective-permute-start(bf16[2,48,4,256]{3,2,1,0:T(4,128)(2,1)S(1)} %get-tuple-element.70), channel_id=1, source_target_pairs={{0,2},{2,4},{4,6},{6,8},{8,10},{10,12},{12,14},{14,0},{1,3},{3,5},... | collective-permute-start | bytes 589832 | tf_op jit(solution)/shard_map/ppermute | solution.py:19
  19.3 33.3 %collective-permute-start.1 = (bf16[2,48,4,256]{3,2,1,0:T(4,128)(2,1)S(1)}, bf16[2,48,4,256]{3,2,1,0:T(4,128)(2,1)S(1)}, u32[]{:S(2)}, u32[]{:S(2)}) collective-permute-start(bf16[2,48,4,256]{3,2,1,0:T(4,128)(2,1)S(1)} %get-tuple-element.71), channel_id=1, source_target_pairs={{2,0},{4,2},{6,4},{8,6},{10,8},{12,10},{14,12},{0,14},{3,1},{5,3},... | collective-permute-start | bytes 589832 | tf_op jit(solution)/shard_map/ppermute | solution.py:21
  35.8 10.2 %all-to-all-start = ((s32[16,2,1]{1,2,0:T(1,128)}), s32[16,2,1]{1,2,0:T(1,128)S(1)}, u32[]{:S(2)}, u32[]{:S(2)}) async-start(s32[16,2,1]{1,2,0:T(1,128)} %bitcast.6), calls=%async_computation | async-start | bytes 16384 | tf_op jit(solution)/shard_map/all_to_all | solution.py:106
  45.9 10.8 %all-to-all-start.2 = ((bf16[32,8,227]{2,1,0:T(8,128)(2,1)}), bf16[32,8,227]{2,1,0:T(8,128)(2,1)S(1)}, u32[]{:S(2)}, u32[]{:S(2)}) async-start(bf16[32,8,227]{2,1,0:T(8,128)(2,1)} %scatter_fusion), calls=%async_computation.2 | async-start | bytes 262144 | tf_op jit(solution)/shard_map/all_to_all | solution.py:105
  51.3 149.5 %all-reduce.4.cloned.1.call-start = ((), (), s32[]{:S(2)}) async-start(), calls=%async_computation.3 | async-start | bytes 999424 | tf_op jit(solution)/shard_map/psum | solution.py:141
  52.8 4.1 %collective-permute-start.2 = (bf16[2,4,40,256]{3,2,1,0:T(8,128)(2,1)S(1)}, bf16[2,4,40,256]{3,2,1,0:T(8,128)(2,1)S(1)}, u32[]{:S(2)}, u32[]{:S(2)}) collective-permute-start(bf16[2,4,40,256]{3,2,1,0:T(8,128)(2,1)S(1)} %get-tuple-element.68), channel_id=1, source_target_pairs={{0,1},{2,3},{4,5},{6,7},{8,9},{10,11},{12,13},{14,15},{16,17},{18,... | collective-permute-start | bytes 491528 | tf_op jit(solution)/shard_map/ppermute | solution.py:19
  54.9 3.3 %collective-permute-start.3 = (bf16[2,4,40,256]{3,2,1,0:T(8,128)(2,1)S(1)}, bf16[2,4,40,256]{3,2,1,0:T(8,128)(2,1)S(1)}, u32[]{:S(2)}, u32[]{:S(2)}) collective-permute-start(bf16[2,4,40,256]{3,2,1,0:T(8,128)(2,1)S(1)} %get-tuple-element.69), channel_id=1, source_target_pairs={{1,0},{3,2},{5,4},{7,6},{9,8},{11,10},{13,12},{15,14},{17,16},{19,... | collective-permute-start | bytes 491528 | tf_op jit(solution)/shard_map/ppermute | solution.py:21
  59.6 1.4 copy-start.7
  59.6 1.4 copy-start.31
  60.6 3.9 %copy-start.1 = (bf16[2,56,40,64]{3,2,1,0:T(8,128)(2,1)}, bf16[2,56,40,64]{3,2,1,0:T(8,128)(2,1)S(1)}, u32[]{:S(2)}) copy-start(bf16[2,56,40,64]{3,2,1,0:T(8,128)(2,1)S(1)} %get-tuple-element.65) | copy-start | bytes 1720324
  60.6 7.1 %copy-start.3 = (bf16[2,56,40,64]{3,2,1,0:T(8,128)(2,1)}, bf16[2,56,40,64]{3,2,1,0:T(8,128)(2,1)S(1)}, u32[]{:S(2)}) copy-start(bf16[2,56,40,64]{3,2,1,0:T(8,128)(2,1)S(1)} %get-tuple-element.66) | copy-start | bytes 1720324
  61.0 3.6 %copy-start.22 = (f32[64]{0:T(128)S(1)}, f32[64]{0:T(128)}, u32[]{:S(2)}) copy-start(f32[64]{0:T(128)} %get-tuple-element.73) | copy-start | bytes 772
  61.0 3.6 %copy-start.23 = (f32[64]{0:T(128)S(1)}, f32[64]{0:T(128)}, u32[]{:S(2)}) copy-start(f32[64]{0:T(128)} %get-tuple-element.74) | copy-start | bytes 772
  61.0 3.6 %copy-start.24 = (f32[64]{0:T(128)S(1)}, f32[64]{0:T(128)}, u32[]{:S(2)}) copy-start(f32[64]{0:T(128)} %get-tuple-element.75) | copy-start | bytes 772
  61.0 3.6 %copy-start.25 = (f32[64]{0:T(128)S(1)}, f32[64]{0:T(128)}, u32[]{:S(2)}) copy-start(f32[64]{0:T(128)} %get-tuple-element.76) | copy-start | bytes 772
  61.0 3.6 %copy-start.26 = (f32[64]{0:T(128)S(1)}, f32[64]{0:T(128)}, u32[]{:S(2)}) copy-start(f32[64]{0:T(128)} %get-tuple-element.77) | copy-start | bytes 772
  61.0 3.6 %copy-start.27 = (f32[64]{0:T(128)S(1)}, f32[64]{0:T(128)}, u32[]{:S(2)}) copy-start(f32[64]{0:T(128)} %get-tuple-element.78) | copy-start | bytes 772
  61.0 3.6 %copy-start.28 = (f32[64]{0:T(128)S(1)}, f32[64]{0:T(128)}, u32[]{:S(2)}) copy-start(f32[64]{0:T(128)} %get-tuple-element.79) | copy-start | bytes 772
  61.0 3.6 %copy-start.29 = (f32[64]{0:T(128)S(1)}, f32[64]{0:T(128)}, u32[]{:S(2)}) copy-start(f32[64]{0:T(128)} %get-tuple-element.80) | copy-start | bytes 772
  61.0 3.6 %copy-start.30 = (f32[64]{0:T(128)S(1)}, f32[64]{0:T(128)}, u32[]{:S(2)}) copy-start(f32[64]{0:T(128)} %get-tuple-element.81) | copy-start | bytes 772
  64.5 10.1 %copy-start.9 = (bf16[2,48,32,64]{3,2,1,0:T(8,128)(2,1)}, bf16[2,48,32,64]{3,2,1,0:T(8,128)(2,1)S(1)}, u32[]{:S(2)}) copy-start(bf16[2,48,32,64]{3,2,1,0:T(8,128)(2,1)S(1)} %fusion.9) | copy-start | bytes 1179652
  64.6 3.2 %copy-start.18 = (f32[64]{0:T(128)S(1)}, f32[64]{0:T(128)}, u32[]{:S(2)}) copy-start(f32[64]{0:T(128)} %get-tuple-element.87) | copy-start | bytes 772
  64.6 3.2 %copy-start.19 = (f32[64]{0:T(128)S(1)}, f32[64]{0:T(128)}, u32[]{:S(2)}) copy-start(f32[64]{0:T(128)} %get-tuple-element.88) | copy-start | bytes 772
  64.6 3.2 %copy-start.20 = (f32[64]{0:T(128)S(1)}, f32[64]{0:T(128)}, u32[]{:S(2)}) copy-start(f32[64]{0:T(128)} %get-tuple-element.89) | copy-start | bytes 772
  64.6 3.2 %copy-start.21 = (f32[64]{0:T(128)S(1)}, f32[64]{0:T(128)}, u32[]{:S(2)}) copy-start(f32[64]{0:T(128)} %get-tuple-element.90) | copy-start | bytes 772
  67.7 6.9 %copy-start.11 = (bf16[2,48,32,64]{3,2,1,0:T(8,128)(2,1)}, bf16[2,48,32,64]{3,2,1,0:T(8,128)(2,1)S(1)}, u32[]{:S(2)}) copy-start(bf16[2,48,32,64]{3,2,1,0:T(8,128)(2,1)S(1)} %fusion.63) | copy-start | bytes 1179652
  71.3 3.4 %copy-start.13 = (bf16[2,48,32,64]{3,2,1,0:T(8,128)(2,1)}, bf16[2,48,32,64]{3,2,1,0:T(8,128)(2,1)S(1)}, u32[]{:S(2)}) copy-start(bf16[2,48,32,64]{3,2,1,0:T(8,128)(2,1)S(1)} %fusion.45) | copy-start | bytes 1179652
  74.6 3.4 %copy-start.15 = (bf16[2,48,32,64]{3,2,1,0:T(8,128)(2,1)}, bf16[2,48,32,64]{3,2,1,0:T(8,128)(2,1)S(1)}, u32[]{:S(2)}) copy-start(bf16[2,48,32,64]{3,2,1,0:T(8,128)(2,1)S(1)} %fusion.27) | copy-start | bytes 1179652
  74.6 6.0 %copy-start.17 = (bf16[256,227]{0,1:T(8,128)(2,1)S(1)}, bf16[256,227]{0,1:T(8,128)(2,1)}, u32[]{:S(2)}) copy-start(bf16[256,227]{0,1:T(8,128)(2,1)} %param.13) | copy-start | bytes 348676
  86.4 5.2 %copy-start.10 = (bf16[2,48,32,64]{3,2,1,0:T(8,128)(2,1)S(1)}, bf16[2,48,32,64]{3,2,1,0:T(8,128)(2,1)}, u32[]{:S(2)}) copy-start(bf16[2,48,32,64]{3,2,1,0:T(8,128)(2,1)} %copy-done.9) | copy-start | bytes 1179652
  86.4 5.2 %copy-start.12 = (bf16[2,48,32,64]{3,2,1,0:T(8,128)(2,1)S(1)}, bf16[2,48,32,64]{3,2,1,0:T(8,128)(2,1)}, u32[]{:S(2)}) copy-start(bf16[2,48,32,64]{3,2,1,0:T(8,128)(2,1)} %copy-done.11) | copy-start | bytes 1179652
  86.4 5.2 %copy-start.14 = (bf16[2,48,32,64]{3,2,1,0:T(8,128)(2,1)S(1)}, bf16[2,48,32,64]{3,2,1,0:T(8,128)(2,1)}, u32[]{:S(2)}) copy-start(bf16[2,48,32,64]{3,2,1,0:T(8,128)(2,1)} %copy-done.13) | copy-start | bytes 1179652
  86.4 5.2 %copy-start.16 = (bf16[2,48,32,64]{3,2,1,0:T(8,128)(2,1)S(1)}, bf16[2,48,32,64]{3,2,1,0:T(8,128)(2,1)}, u32[]{:S(2)}) copy-start(bf16[2,48,32,64]{3,2,1,0:T(8,128)(2,1)} %copy-done.15) | copy-start | bytes 1179652
  90.5 1.2 copy-start.8
  93.8 3.8 %copy-start.2 = (bf16[2,56,40,64]{3,2,1,0:T(8,128)(2,1)S(1)}, bf16[2,56,40,64]{3,2,1,0:T(8,128)(2,1)}, u32[]{:S(2)}) copy-start(bf16[2,56,40,64]{3,2,1,0:T(8,128)(2,1)} %copy-done.1) | copy-start | bytes 1720324
  93.8 3.8 %copy-start.4 = (bf16[2,56,40,64]{3,2,1,0:T(8,128)(2,1)S(1)}, bf16[2,56,40,64]{3,2,1,0:T(8,128)(2,1)}, u32[]{:S(2)}) copy-start(bf16[2,56,40,64]{3,2,1,0:T(8,128)(2,1)} %copy-done.3) | copy-start | bytes 1720324
  96.0 1.7 copy-start.5
Sparse Core Ops, SparseCore 0:
  108.4 92.4 all-reduce.3
where the time goes:
time: 213 us; the launch traced here: 212 us
  blocking collectives  53.6 us (25%)
  other arithmetic  44.3 us (21%)
  waiting for transfers between devices  33.5 us (16%)
  between operations  27 us (13%)
  starting transfers between devices  23.2 us (11%)
  local copies, waits for them, and re-layouts  20.8 us (10%)
  matrix products  9.67 us (5%)
    psum x1, blocking collectives, local(): lax.psum((grad_dw, grad_pw, grad_head, loss_sum), ('lon', 'lat'))  53.6 us
    psum x1, waiting for transfers between devices, local(): lax.psum((grad_dw, grad_pw, grad_head, loss_sum), ('lon', 'lat'))  31 us
    reduce_sum x2, other arithmetic, dilated_grad(): jnp.sum((window.astype(jnp.float32) * group_grad).reshape(-1, group_width...  17.7 us
    another operation x4, other arithmetic  13.3 us
    unnamed x66, local copies, waits for them, and re-layouts  6.59 us
    all_to_all x1, starting transfers between devices, local(): lax.all_to_all(send_count, ('lon', 'lat'), split_axis=0, concat_axis=0, t...  6.27 us
    all_to_all x1, starting transfers between devices, local(): lax.all_to_all(send_tiles, ('lon', 'lat'), split_axis=0, concat_axis=0, t...  5.39 us
    all_to_all x1, starting transfers between devices, local(): lax.all_to_all(send_start, ('lon', 'lat'), split_axis=0, concat_axis=0, t...  5.18 us
  transfers between devices with their start and end apart: 8, of which 4 were waited for; matrix products, arithmetic and copies ran while one was open for 9% of the time, Pallas kernels for 0%

commit v1 on v0

--- a/solution.py
+++ b/solution.py
@@ -139,7 +139,7 @@
     )
     grad_dw = dilated_grad(padded, grad_z, rates, band_rows, block_cols)
     grad_dw, grad_pw, grad_head, loss_sum = lax.psum(
-        (grad_dw, grad_pw, grad_head, loss_sum), ("lon", "lat")
+        lax.psum((grad_dw, grad_pw, grad_head, loss_sum), "lat"), "lon"
     )
     return (grad_dw, grad_pw, grad_head, (loss_sum / teach_width).reshape(1))
 

time: 213 us -> 208 us (0.977)
  blocking collectives: 53.6 us -> 39.6 us
  other arithmetic: 44.3 us -> 52.3 us
    psum x1 -> x2, blocking collectives: 53.6 us -> 39.6 us  [the longest x1 35 us: local(): lax.psum(lax.psum((grad_dw, grad_pw, grad_head, loss_sum), 'lat'), 'lon')]
    reduce_sum x2, other arithmetic: 17.7 us -> 25.6 us  [dilated_grad(): jnp.sum((window.astype(jnp.float32) * group_grad).reshape(-1, group_width...]
    unnamed x66 -> x60, local copies, waits for them, and re-layouts: 6.59 us -> 4.91 us
    psum x1 -> x2, waiting for transfers between devices: 31 us -> 30.5 us  [the longest x1 29 us: local(): lax.psum(lax.psum((grad_dw, grad_pw, grad_head, loss_sum), 'lat'), 'lon')]
  transfers between devices with their start and end apart: 8 -> 9, of which waited for: 4 -> 5; matrix products, arithmetic and copies ran while one was open for 9% -> 18% of each run, Pallas kernels for 0% -> 0%
where the time goes in v1:
time: 208 us; the launch traced here: 205 us
  other arithmetic  52.3 us (25%)
  blocking collectives  39.6 us (19%)
  waiting for transfers between devices  33 us (16%)
  between operations  27 us (13%)
  starting transfers between devices  23.3 us (11%)
  local copies, waits for them, and re-layouts  19.1 us (9%)
  matrix products  11.2 us (5%)
    psum x1, blocking collectives, local(): lax.psum(lax.psum((grad_dw, grad_pw, grad_head, loss_sum), 'lat'), 'lon')  35 us
    psum x1, waiting for transfers between devices, local(): lax.psum(lax.psum((grad_dw, grad_pw, grad_head, loss_sum), 'lat'), 'lon')  29 us
    reduce_sum x2, other arithmetic, dilated_grad(): jnp.sum((window.astype(jnp.float32) * group_grad).reshape(-1, group_width...  25.6 us
    another operation x4, other arithmetic  13.3 us
    all_to_all x1, starting transfers between devices, local(): lax.all_to_all(send_count, ('lon', 'lat'), split_axis=0, concat_axis=0, t...  6.27 us
    all_to_all x1, starting transfers between devices, local(): lax.all_to_all(send_tiles, ('lon', 'lat'), split_axis=0, concat_axis=0, t...  5.39 us
    all_to_all x1, starting transfers between devices, local(): lax.all_to_all(send_start, ('lon', 'lat'), split_axis=0, concat_axis=0, t...  5.18 us
    unnamed x60, local copies, waits for them, and re-layouts  4.91 us
  transfers between devices with their start and end apart: 9, of which 5 were waited for; matrix products, arithmetic and copies ran while one was open for 18% of the time, Pallas kernels for 0%

profile of v1, /device:TPU:8, one launch (start us, length us, event | category | flops | bytes accessed | tf_op | source)
XLA Modules:
  0.0 205.4 jit_solution(5340201135564278929)
XLA Ops:
  7.2 1.0 convert_reduce_fusion
  8.2 0.7 fusion.86
  8.8 0.8 scatter_custom_fusion.1
  9.6 0.7 all_to_all.17
  10.3 6.3 %all-to-all-start.1 = ((s32[16,2,1]{1,2,0:T(1,128)}), s32[16,2,1]{1,2,0:T(1,128)S(1)}, u32[]{:S(2)}, u32[]{:S(2)}) async-start(s32[16,2,1]{1,2,0:T(1,128)} %bitcast.8), calls=%async_computation.1 | async-start | bytes 16384 | tf_op jit(solution)/shard_map/all_to_all | solution.py:107
  16.5 1.3 fusion.94
  17.8 1.5 collective-permute-start
  19.3 1.5 collective-permute-start.1
  20.8 1.4 fusion.95
  32.8 0.7 convert_element_type.185
  33.5 0.1 slice_bitcast_fusion.34
  33.5 0.7 slice_bitcast_fusion.35
  34.2 0.8 scatter_custom_fusion
  35.1 0.7 all_to_all.15
  35.8 5.2 %all-to-all-start = ((s32[16,2,1]{1,2,0:T(1,128)}), s32[16,2,1]{1,2,0:T(1,128)S(1)}, u32[]{:S(2)}, u32[]{:S(2)}) async-start(s32[16,2,1]{1,2,0:T(1,128)} %bitcast.6), calls=%async_computation | async-start | bytes 16384 | tf_op jit(solution)/shard_map/all_to_all | solution.py:106
  41.0 0.7 broadcast_in_dim.15
  41.6 2.3 %scatter_fusion = bf16[32,8,227]{2,1,0:T(8,128)(2,1)} fusion(bf16[32,8,227]{2,1,0:T(8,128)(2,1)} %broadcast_in_dim.15, s32[16]{0:T(128)S(1)} %fusion.86, bf16[16,8,227]{2,1,0:T(8,128)(2,1)} %param.14), kind=kCustom, calls=%fused_computation.3 | custom fusion | bytes 174400 | tf_op jit(solution)/shard_map/scatter | solution.py:100
  43.9 0.6 broadcast.181
  44.5 0.6 reduce.43
  45.2 0.1 lt.50
  45.2 0.7 all-to-all-done
  45.9 5.4 %all-to-all-start.2 = ((bf16[32,8,227]{2,1,0:T(8,128)(2,1)}), bf16[32,8,227]{2,1,0:T(8,128)(2,1)S(1)}, u32[]{:S(2)}, u32[]{:S(2)}) async-start(bf16[32,8,227]{2,1,0:T(8,128)(2,1)} %scatter_fusion), calls=%async_computation.2 | async-start | bytes 262144 | tf_op jit(solution)/shard_map/all_to_all | solution.py:105
  51.3 0.0 all-reduce.9.cloned.1.call-start
  51.4 0.6 reduce.42
  52.0 0.1 add.563
  52.1 0.1 iota_add_fusion
  52.2 0.1 fusion.85
  52.3 0.1 add.567
  52.4 0.1 select_multiply_fusion
  52.4 0.1 div.43
  52.5 0.1 mul.598
  52.7 0.2 pad_maximum_fusion.4
  52.8 2.1 %collective-permute-start.2 = (bf16[2,4,40,256]{3,2,1,0:T(8,128)(2,1)S(1)}, bf16[2,4,40,256]{3,2,1,0:T(8,128)(2,1)S(1)}, u32[]{:S(2)}, u32[]{:S(2)}) collective-permute-start(bf16[2,4,40,256]{3,2,1,0:T(8,128)(2,1)S(1)} %get-tuple-element.72), channel_id=1, source_target_pairs={{0,1},{2,3},{4,5},{6,7},{8,9},{10,11},{12,13},{14,15},{16,17},{18,... | collective-permute-start | bytes 491528 | tf_op jit(solution)/shard_map/ppermute | solution.py:19
  54.9 1.3 collective-permute-start.3
  56.2 0.5 all-to-all-done.2
  56.8 0.1 copy.19
  56.9 1.3 collective-permute-done.3
  58.2 1.4 pad_maximum_fusion
  59.6 1.0 fusion.93
  60.6 0.3 copy-done.4
  61.0 3.5 %fusion.9 = bf16[2,48,32,64]{3,2,1,0:T(8,128)(2,1)S(1)} fusion(f32[64]{0:T(128)S(1)} %get-tuple-element.105, f32[64]{0:T(128)S(1)} %get-tuple-element.106, f32[64]{0:T(128)S(1)} %get-tuple-element.107, f32[64]{0:T(128)S(1)} %get-tuple-element.108, f32[64]{0:T(128)S(1)} %get-tuple-element.109, f32[64]{0:T(128)S(1)} %get-tuple-element.110, ...), kind=kLoop, calls=%fused_computation.90 | loop fusion | flops 5308416 | bytes 3934480 | tf_op jit(solution)/shard_map/convert.9
  64.6 3.1 %fusion.63 = bf16[2,48,32,64]{3,2,1,0:T(8,128)(2,1)S(1)} fusion(f32[64]{0:T(128)S(1)} %copy-done.19, f32[64]{0:T(128)S(1)} %copy-done.20, f32[64]{0:T(128)S(1)} %copy-done.21, f32[64]{0:T(128)S(1)} %copy-done.22, f32[64]{0:T(128)S(1)} %copy-done.23, f32[64]{0:T(128)S(1)} %copy-done.24, f32[64]{0:T(128)S(1)} %copy-done.25, f32[64]{0:T(128)S(1)} %copy-done.26, ...), kind=kLoop, calls=%fused_computation.144 | loop fusion | flops 5308416 | bytes 3934480 | tf_op jit(solution)/shard_map/convert.6
  67.8 3.5 %fusion.45 = bf16[2,48,32,64]{3,2,1,0:T(8,128)(2,1)S(1)} fusion(f32[64]{0:T(128)S(1)} %get-tuple-element.86, f32[64]{0:T(128)S(1)} %get-tuple-element.87, f32[64]{0:T(128)S(1)} %get-tuple-element.88, f32[64]{0:T(128)S(1)} %get-tuple-element.89, f32[64]{0:T(128)S(1)} %get-tuple-element.90, f32[64]{0:T(128)S(1)} %copy-done.15, f32[64]{0:T(128)S(1)} %copy-done.16, ...), kind=kLoop, calls=%fused_computation.126 | loop fusion | flops 5308416 | bytes 3934480 | tf_op jit(solution)/shard_map/convert.7
  71.3 3.3 %fusion.27 = bf16[2,48,32,64]{3,2,1,0:T(8,128)(2,1)S(1)} fusion(f32[64]{0:T(128)S(1)} %get-tuple-element.96, f32[64]{0:T(128)S(1)} %get-tuple-element.97, f32[64]{0:T(128)S(1)} %get-tuple-element.98, f32[64]{0:T(128)S(1)} %get-tuple-element.99, f32[64]{0:T(128)S(1)} %get-tuple-element.100, f32[64]{0:T(128)S(1)} %get-tuple-element.101, ...), kind=kLoop, calls=%fused_computation.108 | loop fusion | flops 5308416 | bytes 3934480 | tf_op jit(solution)/shard_map/convert.8
  74.7 3.4 %fusion = (bf16[3072,256]{1,0:T(8,128)(2,1)}, f32[3072,256]{1,0:T(8,128)}) fusion(bf16[2,48,32,256]{3,2,1,0:T(8,128)(2,1)S(1)} %copy-done.4, bf16[256,256]{1,0:T(8,128)(2,1)S(1)} %copy-done, bf16[3072,64]{1,0:T(8,128)(2,1)S(1)} %bitcast.171, bf16[3072,64]{1,0:T(8,128)(2,1)S(1)} %bitcast.173, bf16[3072,64]{1,0:T(8,128)(2,1)S(1)} %bitcast.175, ...), kind=kOutput, calls=%fused_computation.6 | convolution fusion | flops 414449664 | bytes 7995392 | tf_op jit(solution)/shard_map/dot_general | solution.py:86
  78.0 2.6 %gather_fusion = bf16[256,256]{1,0:T(8,128)(2,1)S(1)} fusion(bf16[3072,256]{1,0:T(8,128)(2,1)} %get-tuple-element.118, s32[1024]{0:T(1024)S(1)} %pad_clamp_fusion), kind=kCustom, calls=%fused_computation | custom fusion | bytes 263168 | tf_op jit(solution)/shard_map/gather | solution.py:122
  80.6 0.9 fusion.75
  81.5 0.9 fusion.76
  82.4 0.2 fusion.77
  82.6 3.8 %scatter_custom_fusion.3 = f32[3072,256]{1,0:T(8,128)} fusion(s32[256]{0:T(256)S(1)} %bitcast.178, f32[256,256]{1,0:T(8,128)S(1)} %fusion.77, f32[]{:T(128)} %constant.101.clone.1), kind=kCustom, calls=%fused_computation.155 | custom fusion | flops 65536 | bytes 3145732 | tf_op jit(solution)/shard_map/scatter-add | solution.py:131
  86.4 4.0 %multiply_convert_fusion = bf16[3072,256]{1,0:T(8,128)(2,1)S(1)} fusion(f32[3072,256]{1,0:T(8,128)} %get-tuple-element.119, f32[3072,256]{1,0:T(8,128)} %scatter_custom_fusion.3), kind=kLoop, calls=%fused_computation.7 | loop fusion | flops 7077888 | bytes 7864320 | tf_op jit(solution)/shard_map/convert_element_type | solution.py:133
  90.5 1.1 copy-done.5
  91.6 2.2 %fusion.91 = f32[256,256]{1,0:T(8,128)} fusion(bf16[3072,256]{1,0:T(8,128)(2,1)S(1)} %multiply_convert_fusion, bf16[3072,64]{1,0:T(8,128)(2,1)S(1)} %bitcast.172, bf16[3072,64]{1,0:T(8,128)(2,1)S(1)} %bitcast.174, bf16[3072,64]{1,0:T(8,128)(2,1)S(1)} %bitcast.176, bf16[3072,64]{1,0:T(8,128)(2,1)S(1)} %bitcast.170), kind=kOutput, calls=%fused_computation.232 | convolution fusion | flops 408944640 | bytes 3407872 | tf_op jit(solution)/shard_map/dot_general | solution.py:134
  93.8 3.7 %fusion.96 = f32[3072,256]{1,0:T(8,128)} fusion(bf16[3072,256]{1,0:T(8,128)(2,1)} %copy-done.5, bf16[256,256]{1,0:T(8,128)(2,1)S(1)} %copy-done), kind=kOutput, calls=%fused_computation.237 | convolution fusion | flops 402653184 | bytes 4849664 | tf_op jit(solution)/shard_map/dot_general | solution.py:137
  97.5 0.0 all-reduce.7.cloned.1.call-start
  97.5 18.5 %fusion.18 = (f32[64]{0:T(128)S(1)}, f32[64]{0:T(128)S(1)}, f32[64]{0:T(128)S(1)}, f32[64]{0:T(128)S(1)}, f32[64]{0:T(128)S(1)}, /*index=5*/f32[64]{0:T(128)S(1)...) fusion(f32[2,48,32,256]{3,2,1,0:T(8,128)} %bitcast.167, ...), kind=kLoop, calls=%fused_computation.99 | loop fusion | flops 14154240 | bytes 11802672 | tf_op jit(solution)/shard_map/reduce_sum | solution.py:66
  116.1 1.5 all-reduce.9.cloned.1.call-done
  117.6 7.1 %fusion.36 = (f32[64]{0:T(128)S(1)}, f32[64]{0:T(128)S(1)}, f32[64]{0:T(128)S(1)}, f32[64]{0:T(128)S(1)}, f32[64]{0:T(128)S(1)}, /*index=5*/f32[64]{0:T(128)S(1)...) fusion(f32[2,48,32,256]{3,2,1,0:T(8,128)} %bitcast.168, ...), kind=kLoop, calls=%fused_computation.117 | loop fusion | flops 7077120 | bytes 7867408 | tf_op jit(solution)/shard_map/reduce_sum | solution.py:66
  124.8 0.1 pad_maximum_fusion.5
  124.9 4.6 %all-reduce.2 = (f32[9,256]{1,0:T(8,128)S(1)}, f32[]{:T(128)}) all-reduce(f32[9,256]{1,0:T(8,128)S(1)} %pad_maximum_fusion.5, f32[]{:T(128)} %get-tuple-element.120), channel_id=1, replica_groups=mesh['groups'=2,'lon'=8,'lat'=2] {'lat'}, use_global_device_ids=true, to_apply=%region_41.42 | all-reduce | flops 2305 | bytes 18440 | tf_op jit(solution)/shard_map/psum | solution.py:142
  129.5 35.0 %all-reduce = (f32[9,256]{1,0:T(8,128)}, f32[]{:T(128)}) all-reduce(f32[9,256]{1,0:T(8,128)S(1)} %get-tuple-element.44, f32[]{:T(128)} %get-tuple-element.45), channel_id=1, replica_groups=mesh['groups'=2,'lon'=8,'lat'=2] {'lon'}, use_global_device_ids=true, to_apply=%region_42.43 | all-reduce | flops 2305 | bytes 18440 | tf_op jit(solution)/shard_map/psum | solution.py:141
  165.1 29.0 %all-reduce.7.cloned.1.call-done = (f32[256,256]{1,0:T(8,128)}, f32[256,227]{0,1:T(8,128)}) async-done(((f32[256,256]{1,0:T(8,128)}, f32[256,227]{0,1:T(8,128)}), (f32[256,256]{1,0:T(8,128)}, f32[256,227]{0,1:T(8,128)})) %all-reduce.7.cloned.1.call-update) | async-done | bytes 494608 | tf_op jit(solution)/shard_map/psum | solution.py:141
  194.1 1.7 copy.25
  195.8 1.6 copy.26
  (69 shorter events, 0.4 us)
Async XLA Ops:
  7.2 67.5 %copy-start = (bf16[256,256]{1,0:T(8,128)(2,1)S(1)}, bf16[256,256]{1,0:T(8,128)(2,1)}, u32[]{:S(2)}) copy-start(bf16[256,256]{1,0:T(8,128)(2,1)} %param.12) | copy-start | bytes 393220
  7.2 45.5 %copy-start.3 = (bf16[2,48,32,256]{3,2,1,0:T(8,128)(2,1)S(1)}, bf16[2,48,32,256]{3,2,1,0:T(8,128)(2,1)}, u32[]{:S(2)}) copy-start(bf16[2,48,32,256]{3,2,1,0:T(8,128)(2,1)} %param.9) | copy-start | bytes 4718596
  10.3 25.5 %all-to-all-start.1 = ((s32[16,2,1]{1,2,0:T(1,128)}), s32[16,2,1]{1,2,0:T(1,128)S(1)}, u32[]{:S(2)}, u32[]{:S(2)}) async-start(s32[16,2,1]{1,2,0:T(1,128)} %bitcast.8), calls=%async_computation.1 | async-start | bytes 16384 | tf_op jit(solution)/shard_map/all_to_all | solution.py:107
  17.8 34.8 %collective-permute-start = (bf16[2,48,4,256]{3,2,1,0:T(4,128)(2,1)S(1)}, bf16[2,48,4,256]{3,2,1,0:T(4,128)(2,1)S(1)}, u32[]{:S(2)}, u32[]{:S(2)}) collective-permute-start(bf16[2,48,4,256]{3,2,1,0:T(4,128)(2,1)S(1)} %get-tuple-element.74), channel_id=1, source_target_pairs={{0,2},{2,4},{4,6},{6,8},{8,10},{10,12},{12,14},{14,0},{1,3},{3,5},... | collective-permute-start | bytes 589832 | tf_op jit(solution)/shard_map/ppermute | solution.py:19
  19.3 33.3 %collective-permute-start.1 = (bf16[2,48,4,256]{3,2,1,0:T(4,128)(2,1)S(1)}, bf16[2,48,4,256]{3,2,1,0:T(4,128)(2,1)S(1)}, u32[]{:S(2)}, u32[]{:S(2)}) collective-permute-start(bf16[2,48,4,256]{3,2,1,0:T(4,128)(2,1)S(1)} %get-tuple-element.75), channel_id=1, source_target_pairs={{2,0},{4,2},{6,4},{8,6},{10,8},{12,10},{14,12},{0,14},{3,1},{5,3},... | collective-permute-start | bytes 589832 | tf_op jit(solution)/shard_map/ppermute | solution.py:21
  35.8 10.2 %all-to-all-start = ((s32[16,2,1]{1,2,0:T(1,128)}), s32[16,2,1]{1,2,0:T(1,128)S(1)}, u32[]{:S(2)}, u32[]{:S(2)}) async-start(s32[16,2,1]{1,2,0:T(1,128)} %bitcast.6), calls=%async_computation | async-start | bytes 16384 | tf_op jit(solution)/shard_map/all_to_all | solution.py:106
  45.9 10.8 %all-to-all-start.2 = ((bf16[32,8,227]{2,1,0:T(8,128)(2,1)}), bf16[32,8,227]{2,1,0:T(8,128)(2,1)S(1)}, u32[]{:S(2)}, u32[]{:S(2)}) async-start(bf16[32,8,227]{2,1,0:T(8,128)(2,1)} %scatter_fusion), calls=%async_computation.2 | async-start | bytes 262144 | tf_op jit(solution)/shard_map/all_to_all | solution.py:105
  51.3 66.2 %all-reduce.9.cloned.1.call-start = ((), (), s32[]{:S(2)}) async-start(), calls=%async_computation.4 | async-start | bytes 999424 | tf_op jit(solution)/shard_map/psum | solution.py:142
  52.8 4.1 %collective-permute-start.2 = (bf16[2,4,40,256]{3,2,1,0:T(8,128)(2,1)S(1)}, bf16[2,4,40,256]{3,2,1,0:T(8,128)(2,1)S(1)}, u32[]{:S(2)}, u32[]{:S(2)}) collective-permute-start(bf16[2,4,40,256]{3,2,1,0:T(8,128)(2,1)S(1)} %get-tuple-element.72), channel_id=1, source_target_pairs={{0,1},{2,3},{4,5},{6,7},{8,9},{10,11},{12,13},{14,15},{16,17},{18,... | collective-permute-start | bytes 491528 | tf_op jit(solution)/shard_map/ppermute | solution.py:19
  54.9 3.3 %collective-permute-start.3 = (bf16[2,4,40,256]{3,2,1,0:T(8,128)(2,1)S(1)}, bf16[2,4,40,256]{3,2,1,0:T(8,128)(2,1)S(1)}, u32[]{:S(2)}, u32[]{:S(2)}) collective-permute-start(bf16[2,4,40,256]{3,2,1,0:T(8,128)(2,1)S(1)} %get-tuple-element.73), channel_id=1, source_target_pairs={{1,0},{3,2},{5,4},{7,6},{9,8},{11,10},{13,12},{15,14},{17,16},{19,... | collective-permute-start | bytes 491528 | tf_op jit(solution)/shard_map/ppermute | solution.py:21
  59.6 1.4 copy-start.4
  59.6 1.4 copy-start.28
  60.6 3.9 %copy-start.1 = (bf16[2,56,40,64]{3,2,1,0:T(8,128)(2,1)}, bf16[2,56,40,64]{3,2,1,0:T(8,128)(2,1)S(1)}, u32[]{:S(2)}) copy-start(bf16[2,56,40,64]{3,2,1,0:T(8,128)(2,1)S(1)} %get-tuple-element.69) | copy-start | bytes 1720324
  60.6 7.1 %copy-start.2 = (bf16[2,56,40,64]{3,2,1,0:T(8,128)(2,1)}, bf16[2,56,40,64]{3,2,1,0:T(8,128)(2,1)S(1)}, u32[]{:S(2)}) copy-start(bf16[2,56,40,64]{3,2,1,0:T(8,128)(2,1)S(1)} %get-tuple-element.70) | copy-start | bytes 1720324
  61.0 3.6 %copy-start.19 = (f32[64]{0:T(128)S(1)}, f32[64]{0:T(128)}, u32[]{:S(2)}) copy-start(f32[64]{0:T(128)} %get-tuple-element.77) | copy-start | bytes 772
  61.0 3.6 %copy-start.20 = (f32[64]{0:T(128)S(1)}, f32[64]{0:T(128)}, u32[]{:S(2)}) copy-start(f32[64]{0:T(128)} %get-tuple-element.78) | copy-start | bytes 772
  61.0 3.6 %copy-start.21 = (f32[64]{0:T(128)S(1)}, f32[64]{0:T(128)}, u32[]{:S(2)}) copy-start(f32[64]{0:T(128)} %get-tuple-element.79) | copy-start | bytes 772
  61.0 3.6 %copy-start.22 = (f32[64]{0:T(128)S(1)}, f32[64]{0:T(128)}, u32[]{:S(2)}) copy-start(f32[64]{0:T(128)} %get-tuple-element.80) | copy-start | bytes 772
  61.0 3.6 %copy-start.23 = (f32[64]{0:T(128)S(1)}, f32[64]{0:T(128)}, u32[]{:S(2)}) copy-start(f32[64]{0:T(128)} %get-tuple-element.81) | copy-start | bytes 772
  61.0 3.6 %copy-start.24 = (f32[64]{0:T(128)S(1)}, f32[64]{0:T(128)}, u32[]{:S(2)}) copy-start(f32[64]{0:T(128)} %get-tuple-element.82) | copy-start | bytes 772
  61.0 3.6 %copy-start.25 = (f32[64]{0:T(128)S(1)}, f32[64]{0:T(128)}, u32[]{:S(2)}) copy-start(f32[64]{0:T(128)} %get-tuple-element.83) | copy-start | bytes 772
  61.0 3.6 %copy-start.26 = (f32[64]{0:T(128)S(1)}, f32[64]{0:T(128)}, u32[]{:S(2)}) copy-start(f32[64]{0:T(128)} %get-tuple-element.84) | copy-start | bytes 772
  61.0 3.6 %copy-start.27 = (f32[64]{0:T(128)S(1)}, f32[64]{0:T(128)}, u32[]{:S(2)}) copy-start(f32[64]{0:T(128)} %get-tuple-element.85) | copy-start | bytes 772
  64.5 10.1 %copy-start.6 = (bf16[2,48,32,64]{3,2,1,0:T(8,128)(2,1)}, bf16[2,48,32,64]{3,2,1,0:T(8,128)(2,1)S(1)}, u32[]{:S(2)}) copy-start(bf16[2,48,32,64]{3,2,1,0:T(8,128)(2,1)S(1)} %fusion.9) | copy-start | bytes 1179652
  64.6 3.2 %copy-start.15 = (f32[64]{0:T(128)S(1)}, f32[64]{0:T(128)}, u32[]{:S(2)}) copy-start(f32[64]{0:T(128)} %get-tuple-element.91) | copy-start | bytes 772
  64.6 3.2 %copy-start.16 = (f32[64]{0:T(128)S(1)}, f32[64]{0:T(128)}, u32[]{:S(2)}) copy-start(f32[64]{0:T(128)} %get-tuple-element.92) | copy-start | bytes 772
  64.6 3.2 %copy-start.17 = (f32[64]{0:T(128)S(1)}, f32[64]{0:T(128)}, u32[]{:S(2)}) copy-start(f32[64]{0:T(128)} %get-tuple-element.93) | copy-start | bytes 772
  64.6 3.2 %copy-start.18 = (f32[64]{0:T(128)S(1)}, f32[64]{0:T(128)}, u32[]{:S(2)}) copy-start(f32[64]{0:T(128)} %get-tuple-element.94) | copy-start | bytes 772
  67.7 6.9 %copy-start.8 = (bf16[2,48,32,64]{3,2,1,0:T(8,128)(2,1)}, bf16[2,48,32,64]{3,2,1,0:T(8,128)(2,1)S(1)}, u32[]{:S(2)}) copy-start(bf16[2,48,32,64]{3,2,1,0:T(8,128)(2,1)S(1)} %fusion.63) | copy-start | bytes 1179652
  71.3 3.4 %copy-start.10 = (bf16[2,48,32,64]{3,2,1,0:T(8,128)(2,1)}, bf16[2,48,32,64]{3,2,1,0:T(8,128)(2,1)S(1)}, u32[]{:S(2)}) copy-start(bf16[2,48,32,64]{3,2,1,0:T(8,128)(2,1)S(1)} %fusion.45) | copy-start | bytes 1179652
  74.6 3.4 %copy-start.12 = (bf16[2,48,32,64]{3,2,1,0:T(8,128)(2,1)}, bf16[2,48,32,64]{3,2,1,0:T(8,128)(2,1)S(1)}, u32[]{:S(2)}) copy-start(bf16[2,48,32,64]{3,2,1,0:T(8,128)(2,1)S(1)} %fusion.27) | copy-start | bytes 1179652
  74.6 6.0 %copy-start.14 = (bf16[256,227]{0,1:T(8,128)(2,1)S(1)}, bf16[256,227]{0,1:T(8,128)(2,1)}, u32[]{:S(2)}) copy-start(bf16[256,227]{0,1:T(8,128)(2,1)} %param.13) | copy-start | bytes 348676
  86.4 5.2 %copy-start.7 = (bf16[2,48,32,64]{3,2,1,0:T(8,128)(2,1)S(1)}, bf16[2,48,32,64]{3,2,1,0:T(8,128)(2,1)}, u32[]{:S(2)}) copy-start(bf16[2,48,32,64]{3,2,1,0:T(8,128)(2,1)} %copy-done.6) | copy-start | bytes 1179652
  86.4 5.2 %copy-start.9 = (bf16[2,48,32,64]{3,2,1,0:T(8,128)(2,1)S(1)}, bf16[2,48,32,64]{3,2,1,0:T(8,128)(2,1)}, u32[]{:S(2)}) copy-start(bf16[2,48,32,64]{3,2,1,0:T(8,128)(2,1)} %copy-done.8) | copy-start | bytes 1179652
  86.4 5.2 %copy-start.11 = (bf16[2,48,32,64]{3,2,1,0:T(8,128)(2,1)S(1)}, bf16[2,48,32,64]{3,2,1,0:T(8,128)(2,1)}, u32[]{:S(2)}) copy-start(bf16[2,48,32,64]{3,2,1,0:T(8,128)(2,1)} %copy-done.10) | copy-start | bytes 1179652
  86.4 5.2 %copy-start.13 = (bf16[2,48,32,64]{3,2,1,0:T(8,128)(2,1)S(1)}, bf16[2,48,32,64]{3,2,1,0:T(8,128)(2,1)}, u32[]{:S(2)}) copy-start(bf16[2,48,32,64]{3,2,1,0:T(8,128)(2,1)} %copy-done.12) | copy-start | bytes 1179652
  90.5 1.1 copy-start.5
  97.5 96.6 %all-reduce.7.cloned.1.call-start = ((), (), s32[]{:S(2)}) async-start(), calls=%async_computation.3 | async-start | bytes 999424 | tf_op jit(solution)/shard_map/psum | solution.py:141
Sparse Core Ops, SparseCore 0:
  97.6 19.8 all-reduce.8
  121.1 72.9 all-reduce.6
